TPU v7x, 32 devices: a whole 2x2x4 slice. The times are simulated.
32 devices in a mesh: basis: 2 (over x), eig: 8 (over z, y), chan: 2 (over core).
Axes of the slice: x: 2, y: 2, z: 4, core: 2. Of those that a mesh axis runs over, the one named last changes fastest.
Arguments:
- eigvecs: bfloat16 [512, 5120], P('eig', 'basis'), may hold values from -6 to 6
- boundary: bfloat16 [5120, 4096], P('basis', 'chan'), may hold values from -0.3125 to 0.3125
- block_sizes: int32 [16], replicated, may hold values from 256 to 768, as said below
- target_of_channel: int32 [4096], P('chan'), may hold values from 0 to 15, as said below
- poles: float32 [512], replicated, may hold values from -4 to 4, as said below
- energies: float32 [16], P('basis'), may hold values from -0.25 to 0.25
Outputs:
- rmatrix: float32 [16, 4096, 4096], P('basis', 'chan', 'eig')
Inputs may be any that keep to these rules, and one draw needn't show every extreme that they name: `poles`: every pole lies 0.5 or more away from zero, with both signs present. `block_sizes`: the sizes sum to 5120; every target state's block holds at least 256 basis rows. `target_of_channel`: every target state has exactly 256 channels.
All inputs are finite; a program needn't handle non-finite values.
Results may differ from a plain program's by a relative error of at most 0.0049.
Values may be sent and summed in bfloat16 or wider, within the bound.
No kernel may reach another device: no remote copies, remote signals or barrier semaphores. Data moves between devices by JAX's collectives and lax.ppermute only.
A program may use at most 128 MiB of HBM per device.

v0:
```python
import jax
import jax.numpy as jnp
from jax import lax
from jax.sharding import PartitionSpec as P


def per_device(eigvecs, boundary, block_sizes, target_of_channel, poles, energies):
    rows_here = eigvecs.shape[1]
    block_ends = jnp.cumsum(block_sizes)
    row_ids = lax.axis_index("basis") * rows_here + jnp.arange(rows_here, dtype=jnp.int32)
    owner_of = jnp.sum((block_ends[None, :] <= row_ids[:, None]).astype(jnp.int32), axis=1)
    member = owner_of[:, None] == target_of_channel[None, :]
    masked = jnp.where(member, boundary, jnp.zeros_like(boundary))
    partial_value = jnp.dot(eigvecs, masked, preferred_element_type=jnp.float32)
    amplitudes = lax.psum(partial_value, "basis").astype(jnp.bfloat16)
    all_channels = lax.all_gather(amplitudes, "chan", axis=1, tiled=True)
    own_width = amplitudes.shape[1]
    own_first = lax.axis_index("chan") * own_width
    col_width = all_channels.shape[1] // lax.axis_size("eig")
    col_first = lax.axis_index("eig") * col_width
    factor = poles.shape[0] ** (-0.5)
    weights = 1.0 / (poles[None, :] - energies[:, None])
    panel_in = lax.all_gather(all_channels, "eig", axis=0, tiled=True)
    left_panel = lax.dynamic_slice_in_dim(panel_in, own_first, own_width, 1)
    right_panel = lax.dynamic_slice_in_dim(panel_in, col_first, col_width, 1)
    scaled = (weights[:, :, None] * left_panel[None].astype(jnp.float32)).astype(jnp.bfloat16)
    summed = jnp.einsum("ekc,kd->ecd", scaled, right_panel, preferred_element_type=jnp.float32)
    return summed * factor


def solution(mesh):
    placed = (P("eig", "basis"), P("basis", "chan"), P(), P("chan"), P(), P("basis"))
    return jax.shard_map(
        per_device, mesh=mesh, in_specs=placed, out_specs=P("basis", "chan", "eig"), check_vma=False
    )
```

profile of v0, /device:TPU:0, one launch (start us, length us, event | category | flops | bytes accessed | tf_op | source)
XLA Modules:
  0.0 140.8 jit_solution(5083630222662826893)
XLA Ops:
  6.5 0.0 copy-start
  6.5 0.0 all-gather.2.cloned.1.call-start
  6.5 0.8 copy.11
  7.4 0.1 reduce
  7.5 0.1 convert_reduce_fusion
  7.6 0.0 copy-done
  7.6 0.0 copy-start.1
  7.6 0.0 copy-start.2
  7.6 6.4 %fusion.6 = f32[64,2048]{1,0:T(8,128)S(1)} fusion(bf16[64,2560]{1,0:T(8,128)(2,1)S(1)} %copy-done, bf16[2560,2048]{1,0:T(8,128)(2,1)} %param.7, s32[2048]{0:T(1024)} %param.9, s32[2560]{0:T(1024)S(1)} %convert_reduce_fusion), kind=kOutput, calls=%fused_computation.9 | convolution fusion | flops 681574400 | bytes 11356160 | tf_op jit(solution)/shard_map/dot_general | solution.py:14
  14.0 18.6 %all-reduce.1 = bf16[64,2048]{1,0:T(8,128)(2,1)S(1)} all-reduce(f32[64,2048]{1,0:T(8,128)S(1)} %fusion.6), channel_id=1, replica_groups=mesh['basis'=2,'eig'=8,'chan'=2] {'basis'}, use_global_device_ids=true, to_apply=%region_2.3 | all-reduce | flops 131072 | bytes 786432 | tf_op jit(solution)/shard_map/psum | solution.py:15
  32.6 2.3 %all_gather.6 = bf16[64,4096]{1,0:T(8,128)(2,1)} all-gather(bf16[64,2048]{1,0:T(8,128)(2,1)S(1)} %all-reduce.1), channel_id=1, replica_groups=mesh['basis'=2,'eig'=8,'chan'=2] {'chan'}, dimensions={1}, use_global_device_ids=true | all-gather | bytes 786432 | tf_op jit(solution)/shard_map/all_gather | solution.py:16
  34.9 0.0 all-gather.2.cloned.1.call-update
  35.0 0.0 copy-done.1
  35.0 0.0 copy-done.2
  35.0 0.1 subtract_divide_fusion
  35.1 73.2 %all-gather.2.cloned.1.call-done = bf16[512,4096]{1,0:T(8,128)(2,1)} async-done(((bf16[64,4096]{1,0:T(8,128)(2,1)}), bf16[512,4096]{1,0:T(8,128)(2,1)}) %all-gather.2.cloned.1.call-update) | async-done | bytes 4194320 | tf_op jit(solution)/shard_map/all_gather | solution.py:23
  108.2 4.1 %dynamic-slice_convert_fusion = f32[512,2048]{1,0:T(8,128)} fusion(bf16[512,4096]{1,0:T(8,128)(2,1)} %all-gather.2.cloned.1.call-done, s32[]{:T(128)S(6)} %select_n.11), kind=kLoop, calls=%fused_computation.10 | loop fusion | flops 1048576 | bytes 6291460 | tf_op jit(solution)/shard_map/convert_element_type | solution.py:26
  112.4 5.3 %copy.12 = f32[512,2048]{0,1:T(8,128)} copy(f32[512,2048]{1,0:T(8,128)} %dynamic-slice_convert_fusion) | data formatting | bytes 8388608 | tf_op jit(solution)/shard_map/convert_element_type | solution.py:26
  117.7 16.3 %convolution_multiply_fusion = f32[8,2048,512]{2,1,0:T(8,128)} fusion(f32[512,2048]{0,1:T(8,128)} %copy.12, f32[8,512]{1,0:T(8,128)S(1)} %subtract_divide_fusion, bf16[512,4096]{1,0:T(8,128)(2,1)} %all-gather.2.cloned.1.call-done, s32[]{:T(128)S(6)} %select_n.12), kind=kOutput, calls=%fused_computation.2 | convolution fusion | flops 8615100416 | bytes 38289412 | tf_op jit(solution)/shard_map/ekc,kd->ecd/dot_general | solution.py:27
  (2 shorter events, 0.0 us)
Async XLA Ops:
  6.5 1.1 copy-start
  6.5 101.7 %all-gather.2.cloned.1.call-start = ((), (), s32[]{:S(2)}) async-start(), calls=%async_computation | async-start | bytes 4718592 | tf_op jit(solution)/shard_map/all_gather | solution.py:23
  7.6 27.4 %copy-start.1 = (f32[512]{0:T(512)S(1)}, f32[512]{0:T(512)}, u32[]{:S(2)}) copy-start(f32[512]{0:T(512)} %param.10) | copy-start | bytes 6148
  7.6 27.4 %copy-start.2 = (f32[8]{0:T(128)S(1)}, f32[8]{0:T(128)}, u32[]{:S(2)}) copy-start(f32[8]{0:T(128)} %param.11) | copy-start | bytes 100
Sparse Core Ops, SparseCore 0:
  35.1 73.1 all-gather.1
where the time goes:
time: 141 us
  waiting for transfers between devices  73.2 us (52%)
  matrix products  22.7 us (16%)
  blocking collectives  20.9 us (15%)
  between operations  13.5 us (10%)
  local copies, waits for them, and re-layouts  6.14 us (4%)
  other arithmetic  4.47 us (3%)
    all_gather x1, waiting for transfers between devices, per_device(): panel_in = lax.all_gather(all_channels, 'eig', axis=0, tiled=True)  73.2 us
    psum x1, blocking collectives, per_device(): amplitudes = lax.psum(partial_value, 'basis').astype(jnp.bfloat16)  18.6 us
    dot_general x1, matrix products, per_device(): jnp.einsum('ekc,kd->ecd', scaled, right_panel, preferred_element_type=jnp...  16.3 us
    dot_general x1, matrix products, per_device(): partial_value = jnp.dot(eigvecs, masked, preferred_element_type=jnp.float32)  6.39 us
    convert_element_type x1, local copies, waits for them, and re-layouts, per_device(): left_panel[None].astype(jnp.float32)  5.34 us
    convert_element_type x1, other arithmetic, per_device(): left_panel[None].astype(jnp.float32)  4.13 us
  transfers between devices with their start and end apart: 1, of which 1 were waited for; matrix products, arithmetic and copies ran while one was open for 0% of the time, Pallas kernels for 0%

commit v1 on v0

--- a/solution.py
+++ b/solution.py
@@ -20,7 +20,26 @@
     col_first = lax.axis_index("eig") * col_width
     factor = poles.shape[0] ** (-0.5)
     weights = 1.0 / (poles[None, :] - energies[:, None])
-    panel_in = lax.all_gather(all_channels, "eig", axis=0, tiled=True)
+    size, place, extent = (lax.axis_size("eig"), lax.axis_index("eig"), all_channels.shape[0])
+    ahead = [(i, (i + 1) % size) for i in range(size)]
+    left = [(i, (i - 1) % size) for i in range(size)]
+    result = jnp.zeros(
+        (*all_channels.shape[:0], size * extent, *all_channels.shape[0 + 1 :]), all_channels.dtype
+    )
+    result = lax.dynamic_update_slice_in_dim(result, all_channels, place * extent, axis=0)
+    from_left = from_right = all_channels
+    half = size // 2
+    for turn in range(1, half + 1):
+        from_left = lax.ppermute(from_left, "eig", ahead)
+        result = lax.dynamic_update_slice_in_dim(
+            result, from_left, (place - turn) % size * extent, axis=0
+        )
+        if turn < size - half:
+            from_right = lax.ppermute(from_right, "eig", left)
+            result = lax.dynamic_update_slice_in_dim(
+                result, from_right, (place + turn) % size * extent, axis=0
+            )
+    panel_in = result
     left_panel = lax.dynamic_slice_in_dim(panel_in, own_first, own_width, 1)
     right_panel = lax.dynamic_slice_in_dim(panel_in, col_first, col_width, 1)
     scaled = (weights[:, :, None] * left_panel[None].astype(jnp.float32)).astype(jnp.bfloat16)

time: 141 us -> 146 us (1.035)
  between operations: 13.5 us -> 0.23 us
  starting transfers between devices: 0.01 us -> 12.2 us
  waiting for transfers between devices: 73.2 us -> 77.7 us
  local copies, waits for them, and re-layouts: 6.14 us -> 8.93 us
  other arithmetic: 4.47 us -> 2.88 us
    ppermute x0 -> x7, waiting for transfers between devices: none -> 77.7 us  [the longest x3 41.6 us: per_device(): from_right = lax.ppermute(from_right, 'eig', left)]
    all_gather x1 -> x0, waiting for transfers between devices: 73.2 us -> none  [per_device(): panel_in = lax.all_gather(all_channels, 'eig', axis=0, tiled=True)]
    ppermute x0 -> x7, starting transfers between devices: none -> 12.2 us  [the longest x3 9.72 us: per_device(): from_right = lax.ppermute(from_right, 'eig', left)]
    unnamed x6 -> x8, local copies, waits for them, and re-layouts: 0.02 us -> 1.98 us
    convert_element_type x1, other arithmetic: 4.13 us -> 2.54 us  [per_device(): left_panel[None].astype(jnp.float32)]
  transfers between devices with their start and end apart: 1 -> 7, of which waited for: 1 -> 4; matrix products, arithmetic and copies ran while one was open for 0% -> 1% of each run, Pallas kernels for 0% -> 0%
where the time goes in v1:
time: 146 us; the launch traced here: 145 us
  waiting for transfers between devices  77.7 us (53%)
  matrix products  22.7 us (16%)
  blocking collectives  20.8 us (14%)
  starting transfers between devices  12.2 us (8%)
  local copies, waits for them, and re-layouts  8.93 us (6%)
  other arithmetic  2.88 us (2%)
    ppermute x3, waiting for transfers between devices, per_device(): from_right = lax.ppermute(from_right, 'eig', left)  41.6 us
    ppermute x4, waiting for transfers between devices, per_device(): from_left = lax.ppermute(from_left, 'eig', ahead)  36.1 us
    psum x1, blocking collectives, per_device(): amplitudes = lax.psum(partial_value, 'basis').astype(jnp.bfloat16)  18.6 us
    dot_general x1, matrix products, per_device(): jnp.einsum('ekc,kd->ecd', scaled, right_panel, preferred_element_type=jnp...  16.3 us
    ppermute x3, starting transfers between devices, per_device(): from_right = lax.ppermute(from_right, 'eig', left)  9.72 us
    dot_general x1, matrix products, per_device(): partial_value = jnp.dot(eigvecs, masked, preferred_element_type=jnp.float32)  6.39 us
    convert_element_type x1, local copies, waits for them, and re-layouts, per_device(): left_panel[None].astype(jnp.float32)  5.35 us
  transfers between devices with their start and end apart: 7, of which 4 were waited for; matrix products, arithmetic and copies ran while one was open for 1% of the time, Pallas kernels for 0%

profile of v1, /device:TPU:0, one launch (start us, length us, event | category | flops | bytes accessed | tf_op | source)
XLA Modules:
  0.0 145.4 jit_solution(13631930627231229600)
XLA Ops:
  0.0 0.0 copy-start
  0.0 0.8 copy.11
  0.8 0.1 reduce
  0.9 0.1 convert_reduce_fusion
  1.1 0.0 copy-done
  1.1 0.0 copy-start.2
  1.1 0.0 copy-start.3
  1.1 6.4 %fusion.6 = f32[64,2048]{1,0:T(8,128)S(1)} fusion(bf16[64,2560]{1,0:T(8,128)(2,1)S(1)} %copy-done, bf16[2560,2048]{1,0:T(8,128)(2,1)} %param.7, s32[2048]{0:T(1024)} %param.9, s32[2560]{0:T(1024)S(1)} %convert_reduce_fusion), kind=kOutput, calls=%fused_computation.9 | convolution fusion | flops 681574400 | bytes 11356160 | tf_op jit(solution)/shard_map/dot_general | solution.py:14
  7.5 18.6 %all-reduce.1 = bf16[64,2048]{1,0:T(8,128)(2,1)S(1)} all-reduce(f32[64,2048]{1,0:T(8,128)S(1)} %fusion.6), channel_id=1, replica_groups=mesh['basis'=2,'eig'=8,'chan'=2] {'basis'}, use_global_device_ids=true, to_apply=%region_2.3 | all-reduce | flops 131072 | bytes 786432 | tf_op jit(solution)/shard_map/psum | solution.py:15
  26.1 2.2 %all_gather.3 = bf16[64,4096]{1,0:T(8,128)(2,1)S(1)} all-gather(bf16[64,2048]{1,0:T(8,128)(2,1)S(1)} %all-reduce.1), channel_id=1, replica_groups=mesh['basis'=2,'eig'=8,'chan'=2] {'chan'}, dimensions={1}, use_global_device_ids=true | all-gather | bytes 786432 | tf_op jit(solution)/shard_map/all_gather | solution.py:16
  28.3 4.6 %collective-permute-start.1 = (bf16[64,4096]{1,0:T(8,128)(2,1)S(1)}, bf16[64,4096]{1,0:T(8,128)(2,1)S(1)}, u32[]{:S(2)}, u32[]{:S(2)}) collective-permute-start(bf16[64,4096]{1,0:T(8,128)(2,1)S(1)} %all_gather.3), channel_id=1, source_target_pairs={{0,14},{2,0},{4,2},{6,4},{8,6},{10,8},{12,10},{14,12},{1,15},{3,1}... | collective-permute-start | bytes 1572872 | tf_op jit(solution)/shard_map/ppermute | solution.py:38
  32.8 0.0 collective-permute-start
  32.8 0.0 copy-done.2
  32.8 0.0 copy-done.3
  32.8 0.1 subtract_divide_fusion
  33.0 0.5 broadcast_in_dim.4
  33.6 19.9 %collective-permute-done.1 = bf16[64,4096]{1,0:T(8,128)(2,1)S(1)} collective-permute-done((bf16[64,4096]{1,0:T(8,128)(2,1)S(1)}, bf16[64,4096]{1,0:T(8,128)(2,1)S(1)}, u32[]{:S(2)}, u32[]{:S(2)}) %collective-permute-start.1) | collective-permute-done | bytes 524320 | tf_op jit(solution)/shard_map/ppermute | solution.py:38
  53.5 2.6 %collective-permute-start.3 = (bf16[64,4096]{1,0:T(8,128)(2,1)S(1)}, bf16[64,4096]{1,0:T(8,128)(2,1)S(1)}, u32[]{:S(2)}, u32[]{:S(2)}) collective-permute-start(bf16[64,4096]{1,0:T(8,128)(2,1)S(1)} %collective-permute-done.1), channel_id=1, source_target_pairs={{0,14},{2,0},{4,2},{6,4},{8,6},{10,8},{12,10},{14,12},{1,15},{3,1}... | collective-permute-start | bytes 1572872 | tf_op jit(solution)/shard_map/ppermute | solution.py:38
  56.1 0.0 collective-permute-done
  56.1 0.0 collective-permute-start.2
  56.2 21.7 %collective-permute-done.3 = bf16[64,4096]{1,0:T(8,128)(2,1)S(1)} collective-permute-done((bf16[64,4096]{1,0:T(8,128)(2,1)S(1)}, bf16[64,4096]{1,0:T(8,128)(2,1)S(1)}, u32[]{:S(2)}, u32[]{:S(2)}) %collective-permute-start.3) | collective-permute-done | bytes 524320 | tf_op jit(solution)/shard_map/ppermute | solution.py:38
  77.8 2.6 %collective-permute-start.5 = (bf16[64,4096]{1,0:T(8,128)(2,1)S(1)}, bf16[64,4096]{1,0:T(8,128)(2,1)S(1)}, u32[]{:S(2)}, u32[]{:S(2)}) collective-permute-start(bf16[64,4096]{1,0:T(8,128)(2,1)S(1)} %collective-permute-done.3), channel_id=1, source_target_pairs={{0,14},{2,0},{4,2},{6,4},{8,6},{10,8},{12,10},{14,12},{1,15},{3,1}... | collective-permute-start | bytes 1572872 | tf_op jit(solution)/shard_map/ppermute | solution.py:38
  80.4 0.0 collective-permute-done.2
  80.4 0.0 collective-permute-start.4
  80.5 19.9 %collective-permute-done.4 = bf16[64,4096]{1,0:T(8,128)(2,1)S(1)} collective-permute-done((bf16[64,4096]{1,0:T(8,128)(2,1)S(1)}, bf16[64,4096]{1,0:T(8,128)(2,1)S(1)}, u32[]{:S(2)}, u32[]{:S(2)}) %collective-permute-start.4) | collective-permute-done | bytes 524320 | tf_op jit(solution)/shard_map/ppermute | solution.py:33
  100.4 2.5 %collective-permute-start.6 = (bf16[64,4096]{1,0:T(8,128)(2,1)S(1)}, bf16[64,4096]{1,0:T(8,128)(2,1)S(1)}, u32[]{:S(2)}, u32[]{:S(2)}) collective-permute-start(bf16[64,4096]{1,0:T(8,128)(2,1)S(1)} %collective-permute-done.4), channel_id=1, source_target_pairs={{0,2},{2,4},{4,6},{6,8},{8,10},{10,12},{12,14},{14,0},{1,3},{3,5},... | collective-permute-start | bytes 1572872 | tf_op jit(solution)/shard_map/ppermute | solution.py:33
  102.9 0.0 collective-permute-done.5
  103.0 16.3 %collective-permute-done.6 = bf16[64,4096]{1,0:T(8,128)(2,1)S(1)} collective-permute-done((bf16[64,4096]{1,0:T(8,128)(2,1)S(1)}, bf16[64,4096]{1,0:T(8,128)(2,1)S(1)}, u32[]{:S(2)}, u32[]{:S(2)}) %collective-permute-start.6) | collective-permute-done | bytes 524320 | tf_op jit(solution)/shard_map/ppermute | solution.py:33
  119.3 0.0 copy-start.1
  119.3 2.0 %copy-done.1 = bf16[512,4096]{1,0:T(8,128)(2,1)} copy-done((bf16[512,4096]{1,0:T(8,128)(2,1)}, bf16[512,4096]{1,0:T(8,128)(2,1)S(1)}, u32[]{:S(2)}) %copy-start.1) | copy-done | bytes 4194328
  121.2 2.5 %dynamic-slice_convert_fusion = f32[512,2048]{1,0:T(8,128)} fusion(bf16[512,4096]{1,0:T(8,128)(2,1)S(1)} %constant_dynamic-update-slice_fusion, s32[]{:T(128)S(6)} %select_n.81), kind=kLoop, calls=%fused_computation.10 | loop fusion | flops 1048576 | bytes 6291460 | tf_op jit(solution)/shard_map/convert_element_type | solution.py:45
  123.8 5.3 %copy.12 = f32[512,2048]{0,1:T(8,128)} copy(f32[512,2048]{1,0:T(8,128)} %dynamic-slice_convert_fusion) | data formatting | bytes 8388608 | tf_op jit(solution)/shard_map/convert_element_type | solution.py:45
  129.1 16.3 %convolution_multiply_fusion = f32[8,2048,512]{2,1,0:T(8,128)} fusion(f32[512,2048]{0,1:T(8,128)} %copy.12, f32[8,512]{1,0:T(8,128)S(1)} %subtract_divide_fusion, bf16[512,4096]{1,0:T(8,128)(2,1)} %copy-done.1, s32[]{:T(128)S(6)} %select_n.82), kind=kOutput, calls=%fused_computation.2 | convolution fusion | flops 8615100416 | bytes 38289412 | tf_op jit(solution)/shard_map/ekc,kd->ecd/dot_general | solution.py:46
  (10 shorter events, 0.4 us)
Async XLA Ops:
  0.0 1.1 copy-start
  1.1 31.8 %copy-start.2 = (f32[512]{0:T(512)S(1)}, f32[512]{0:T(512)}, u32[]{:S(2)}) copy-start(f32[512]{0:T(512)} %param.10) | copy-start | bytes 6148
  1.1 31.8 %copy-start.3 = (f32[8]{0:T(128)S(1)}, f32[8]{0:T(128)}, u32[]{:S(2)}) copy-start(f32[8]{0:T(128)} %param.11) | copy-start | bytes 100
  28.3 25.2 %collective-permute-start.1 = (bf16[64,4096]{1,0:T(8,128)(2,1)S(1)}, bf16[64,4096]{1,0:T(8,128)(2,1)S(1)}, u32[]{:S(2)}, u32[]{:S(2)}) collective-permute-start(bf16[64,4096]{1,0:T(8,128)(2,1)S(1)} %all_gather.3), channel_id=1, source_target_pairs={{0,14},{2,0},{4,2},{6,4},{8,6},{10,8},{12,10},{14,12},{1,15},{3,1}... | collective-permute-start | bytes 1572872 | tf_op jit(solution)/shard_map/ppermute | solution.py:38
  32.8 23.2 %collective-permute-start = (bf16[64,4096]{1,0:T(8,128)(2,1)S(1)}, bf16[64,4096]{1,0:T(8,128)(2,1)S(1)}, u32[]{:S(2)}, u32[]{:S(2)}) collective-permute-start(bf16[64,4096]{1,0:T(8,128)(2,1)S(1)} %all_gather.3), channel_id=1, source_target_pairs={{0,2},{2,4},{4,6},{6,8},{8,10},{10,12},{12,14},{14,0},{1,3},{3,5},... | collective-permute-start | bytes 1572872 | tf_op jit(solution)/shard_map/ppermute | solution.py:33
  53.5 24.3 %collective-permute-start.3 = (bf16[64,4096]{1,0:T(8,128)(2,1)S(1)}, bf16[64,4096]{1,0:T(8,128)(2,1)S(1)}, u32[]{:S(2)}, u32[]{:S(2)}) collective-permute-start(bf16[64,4096]{1,0:T(8,128)(2,1)S(1)} %collective-permute-done.1), channel_id=1, source_target_pairs={{0,14},{2,0},{4,2},{6,4},{8,6},{10,8},{12,10},{14,12},{1,15},{3,1}... | collective-permute-start | bytes 1572872 | tf_op jit(solution)/shard_map/ppermute | solution.py:38
  56.1 24.3 %collective-permute-start.2 = (bf16[64,4096]{1,0:T(8,128)(2,1)S(1)}, bf16[64,4096]{1,0:T(8,128)(2,1)S(1)}, u32[]{:S(2)}, u32[]{:S(2)}) collective-permute-start(bf16[64,4096]{1,0:T(8,128)(2,1)S(1)} %collective-permute-done), channel_id=1, source_target_pairs={{0,2},{2,4},{4,6},{6,8},{8,10},{10,12},{12,14},{14,0},{1,3},{3,5},... | collective-permute-start | bytes 1572872 | tf_op jit(solution)/shard_map/ppermute | solution.py:33
  77.8 25.1 %collective-permute-start.5 = (bf16[64,4096]{1,0:T(8,128)(2,1)S(1)}, bf16[64,4096]{1,0:T(8,128)(2,1)S(1)}, u32[]{:S(2)}, u32[]{:S(2)}) collective-permute-start(bf16[64,4096]{1,0:T(8,128)(2,1)S(1)} %collective-permute-done.3), channel_id=1, source_target_pairs={{0,14},{2,0},{4,2},{6,4},{8,6},{10,8},{12,10},{14,12},{1,15},{3,1}... | collective-permute-start | bytes 1572872 | tf_op jit(solution)/shard_map/ppermute | solution.py:38
  80.4 20.0 %collective-permute-start.4 = (bf16[64,4096]{1,0:T(8,128)(2,1)S(1)}, bf16[64,4096]{1,0:T(8,128)(2,1)S(1)}, u32[]{:S(2)}, u32[]{:S(2)}) collective-permute-start(bf16[64,4096]{1,0:T(8,128)(2,1)S(1)} %collective-permute-done.2), channel_id=1, source_target_pairs={{0,2},{2,4},{4,6},{6,8},{8,10},{10,12},{12,14},{14,0},{1,3},{3,5},... | collective-permute-start | bytes 1572872 | tf_op jit(solution)/shard_map/ppermute | solution.py:33
  100.4 18.8 %collective-permute-start.6 = (bf16[64,4096]{1,0:T(8,128)(2,1)S(1)}, bf16[64,4096]{1,0:T(8,128)(2,1)S(1)}, u32[]{:S(2)}, u32[]{:S(2)}) collective-permute-start(bf16[64,4096]{1,0:T(8,128)(2,1)S(1)} %collective-permute-done.4), channel_id=1, source_target_pairs={{0,2},{2,4},{4,6},{6,8},{8,10},{10,12},{12,14},{14,0},{1,3},{3,5},... | collective-permute-start | bytes 1572872 | tf_op jit(solution)/shard_map/ppermute | solution.py:33
  119.3 2.0 %copy-start.1 = (bf16[512,4096]{1,0:T(8,128)(2,1)}, bf16[512,4096]{1,0:T(8,128)(2,1)S(1)}, u32[]{:S(2)}) copy-start(bf16[512,4096]{1,0:T(8,128)(2,1)S(1)} %constant_dynamic-update-slice_fusion) | copy-start | bytes 12582916

commit v2 on v0

--- a/solution.py
+++ b/solution.py
@@ -12,7 +12,7 @@
     member = owner_of[:, None] == target_of_channel[None, :]
     masked = jnp.where(member, boundary, jnp.zeros_like(boundary))
     partial_value = jnp.dot(eigvecs, masked, preferred_element_type=jnp.float32)
-    amplitudes = lax.psum(partial_value, "basis").astype(jnp.bfloat16)
+    amplitudes = jnp.sum(lax.all_gather(partial_value, "basis"), axis=0).astype(jnp.bfloat16)
     all_channels = lax.all_gather(amplitudes, "chan", axis=1, tiled=True)
     own_width = amplitudes.shape[1]
     own_first = lax.axis_index("chan") * own_width

time: 141 us -> 148 us (1.050)
  waiting for transfers between devices: 73.2 us -> 97 us
  blocking collectives: 20.9 us -> 2.31 us
    all_gather x0 -> x1, waiting for transfers between devices: none -> 24.1 us  [per_device(): lax.all_gather(partial_value, 'basis')]
    psum x1 -> x0, blocking collectives: 18.6 us -> none  [per_device(): amplitudes = lax.psum(partial_value, 'basis').astype(jnp.bfloat16)]
  transfers between devices with their start and end apart: 1 -> 2, of which waited for: 1 -> 2; matrix products, arithmetic and copies ran while one was open for 0% -> 0% of each run, Pallas kernels for 0% -> 0%
where the time goes in v2:
time: 148 us
  waiting for transfers between devices  97 us (66%)
  matrix products  23.5 us (16%)
  between operations  13.5 us (9%)
  local copies, waits for them, and re-layouts  6.14 us (4%)
  other arithmetic  5.79 us (4%)
  blocking collectives  2.31 us (2%)
    all_gather x1, waiting for transfers between devices, per_device(): panel_in = lax.all_gather(all_channels, 'eig', axis=0, tiled=True)  72.9 us
    all_gather x1, waiting for transfers between devices, per_device(): lax.all_gather(partial_value, 'basis')  24.1 us
    dot_general x1, matrix products, per_device(): jnp.einsum('ekc,kd->ecd', scaled, right_panel, preferred_element_type=jnp...  16.3 us
    dot_general x1, matrix products, per_device(): partial_value = jnp.dot(eigvecs, masked, preferred_element_type=jnp.float32)  7.18 us
    convert_element_type x1, local copies, waits for them, and re-layouts, per_device(): left_panel[None].astype(jnp.float32)  5.34 us
    convert_element_type x1, other arithmetic, per_device(): left_panel[None].astype(jnp.float32)  4.13 us
  transfers between devices with their start and end apart: 2, of which 2 were waited for; matrix products, arithmetic and copies ran while one was open for 0% of the time, Pallas kernels for 0%

profile of v2, /device:TPU:0, one launch (start us, length us, event | category | flops | bytes accessed | tf_op | source)
XLA Modules:
  0.0 148.2 jit_solution(17495545838618572267)
XLA Ops:
  6.5 0.0 copy-start
  6.5 0.0 all-gather.6.cloned.1.call-start
  6.5 0.8 copy.11
  7.4 0.1 reduce
  7.5 0.1 convert_reduce_fusion
  7.6 0.0 copy-done
  7.6 0.0 copy-start.1
  7.6 0.0 copy-start.2
  7.6 7.2 %fusion.6 = f32[64,2048]{1,0:T(8,128)} fusion(bf16[64,2560]{1,0:T(8,128)(2,1)S(1)} %copy-done, bf16[2560,2048]{1,0:T(8,128)(2,1)} %param.7, s32[2048]{0:T(1024)} %param.9, s32[2560]{0:T(1024)S(1)} %convert_reduce_fusion), kind=kOutput, calls=%fused_computation.9 | convolution fusion | flops 681574400 | bytes 11356160 | tf_op jit(solution)/shard_map/dot_general | solution.py:14
  14.8 0.0 all-gather.6.cloned.1.call-update
  14.8 0.0 all-gather.4.cloned.1.call-start
  14.9 24.1 %all-gather.6.cloned.1.call-done = f32[128,2048]{1,0:T(8,128)} async-done(((f32[64,2048]{1,0:T(8,128)}), f32[128,2048]{1,0:T(8,128)}) %all-gather.6.cloned.1.call-update) | async-done | bytes 1048592 | tf_op jit(solution)/shard_map/all_gather | solution.py:15
  39.0 1.3 reduce_sum.19
  40.3 2.3 %all_gather.14 = bf16[64,4096]{1,0:T(8,128)(2,1)} all-gather(bf16[64,2048]{1,0:T(8,128)(2,1)S(1)} %reduce_sum.19), channel_id=1, replica_groups=mesh['basis'=2,'eig'=8,'chan'=2] {'chan'}, dimensions={1}, use_global_device_ids=true | all-gather | bytes 786432 | tf_op jit(solution)/shard_map/all_gather | solution.py:16
  42.6 0.0 all-gather.4.cloned.1.call-update
  42.6 0.0 copy-done.1
  42.7 0.0 copy-done.2
  42.7 0.1 subtract_divide_fusion
  42.7 72.9 %all-gather.4.cloned.1.call-done = bf16[512,4096]{1,0:T(8,128)(2,1)} async-done(((bf16[64,4096]{1,0:T(8,128)(2,1)}), bf16[512,4096]{1,0:T(8,128)(2,1)}) %all-gather.4.cloned.1.call-update) | async-done | bytes 4194320 | tf_op jit(solution)/shard_map/all_gather | solution.py:23
  115.6 4.1 %dynamic-slice_convert_fusion = f32[512,2048]{1,0:T(8,128)} fusion(bf16[512,4096]{1,0:T(8,128)(2,1)} %all-gather.4.cloned.1.call-done, s32[]{:T(128)S(6)} %select_n.11), kind=kLoop, calls=%fused_computation.10 | loop fusion | flops 1048576 | bytes 6291460 | tf_op jit(solution)/shard_map/convert_element_type | solution.py:26
  119.7 5.3 %copy.12 = f32[512,2048]{0,1:T(8,128)} copy(f32[512,2048]{1,0:T(8,128)} %dynamic-slice_convert_fusion) | data formatting | bytes 8388608 | tf_op jit(solution)/shard_map/convert_element_type | solution.py:26
  125.1 16.3 %convolution_multiply_fusion = f32[8,2048,512]{2,1,0:T(8,128)} fusion(f32[512,2048]{0,1:T(8,128)} %copy.12, f32[8,512]{1,0:T(8,128)S(1)} %subtract_divide_fusion, bf16[512,4096]{1,0:T(8,128)(2,1)} %all-gather.4.cloned.1.call-done, s32[]{:T(128)S(6)} %select_n.12), kind=kOutput, calls=%fused_computation.2 | convolution fusion | flops 8615100416 | bytes 38289412 | tf_op jit(solution)/shard_map/ekc,kd->ecd/dot_general | solution.py:27
  (2 shorter events, 0.0 us)
Async XLA Ops:
  6.5 1.1 copy-start
  6.5 32.4 %all-gather.6.cloned.1.call-start = ((), (), s32[]{:S(2)}) async-start(), calls=%async_computation.1 | async-start | bytes 1572864 | tf_op jit(solution)/shard_map/all_gather | solution.py:15
  7.6 35.1 %copy-start.1 = (f32[512]{0:T(512)S(1)}, f32[512]{0:T(512)}, u32[]{:S(2)}) copy-start(f32[512]{0:T(512)} %param.10) | copy-start | bytes 6148
  7.6 35.0 %copy-start.2 = (f32[8]{0:T(128)S(1)}, f32[8]{0:T(128)}, u32[]{:S(2)}) copy-start(f32[8]{0:T(128)} %param.11) | copy-start | bytes 100
  14.8 100.8 %all-gather.4.cloned.1.call-start = ((), (), s32[]{:S(2)}) async-start(), calls=%async_computation | async-start | bytes 4718592 | tf_op jit(solution)/shard_map/all_gather | solution.py:23
Sparse Core Ops, SparseCore 0:
  14.9 23.9 all-gather.5
  42.8 72.7 all-gather.3
